TPU v7x, 256 devices: a whole 4x4x8 slice. The times are simulated.
256 devices in a mesh: seq: 64 (over z, y, core), tensor: 4 (over x).
Axes of the slice: x: 4, y: 4, z: 8, core: 2. Of those that a mesh axis runs over, the one named last changes fastest.
Arguments:
- new_states: bfloat16 [4, 128, 1024], P(None, None, 'tensor'), may hold values from -6 to 6
- self_query: bfloat16 [1024, 1024], P(None, 'tensor'), may hold values from -0.1875 to 0.1875
- self_key: bfloat16 [1024, 1024], P(None, 'tensor'), may hold values from -0.375 to 0.375
- self_value: bfloat16 [1024, 1024], P(None, 'tensor'), may hold values from -0.1875 to 0.1875
- self_output: bfloat16 [1024, 1024], P('tensor'), may hold values from -0.1875 to 0.1875
- cross_query: bfloat16 [1024, 1024], P(None, 'tensor'), may hold values from -0.1875 to 0.1875
- cross_output: bfloat16 [1024, 1024], P('tensor'), may hold values from -0.1875 to 0.1875
- feed_up: bfloat16 [1024, 4096], P(None, 'tensor'), may hold values from -0.1875 to 0.1875
- feed_down: bfloat16 [4096, 1024], P('tensor'), may hold values from -0.09375 to 0.09375
- norm_self: float32 [1024], replicated, may hold values from 0.25 to 1.75
- norm_cross: float32 [1024], replicated, may hold values from 0.25 to 1.75
- norm_feed: float32 [1024], replicated, may hold values from 0.25 to 1.75
- self_cache: bfloat16 [1536, 2, 128, 1024], P('seq', None, None, 'tensor'), may hold values from -240 to 240
- cross_cache: bfloat16 [128, 2, 512, 1024], P(None, None, 'seq', 'tensor'), may hold values from -240 to 240
- cache_lengths: int32 [128], replicated, may hold values from 1 to 16384, as said below
- page_table: int32 [128, 128], replicated, may hold values from -1 to 1535, as said below
- request_order: int32 [128], replicated, may hold values from 0 to 127, each once
- encoder_lengths: int32 [128], replicated, may hold values from 1 to 512, as said below
Outputs:
- out: bfloat16 [4, 128, 1024], P(None, None, 'tensor')
Inputs may be any that keep to these rules, and one draw needn't show every extreme that they name: `cache_lengths`: one request has exactly 16384 cached tokens. `page_table`: row r holds the slots of request r's pages in order: its first ceil(cache_lengths[r] / 128) entries are slots, page p holding positions p * 128 to (p + 1) * 128 - 1, and no slot appears twice in the table; the other entries are -1. Slot s belongs to seq index s // 24. `encoder_lengths`: one request has exactly 512 encoder positions.
All inputs are finite; a program needn't handle non-finite values.
Results may differ from a plain program's by a relative error of at most 0.014.
The roundings to bfloat16 on the way count: a program that leaves them out, or rounds other values in their place, can miss the bound.
Values may be sent and summed in bfloat16 or wider, within the bound.
No kernel may reach another device: no remote copies, remote signals or barrier semaphores. Data moves between devices by JAX's collectives and lax.ppermute only.
A program may use at most 64 MiB of HBM per device.

v0:
```python
import jax
import jax.numpy as jnp
from jax import lax
from jax.sharding import PartitionSpec as P

HEAD_DIM = 64
EPSILON = 1e-05
NEG_FILL = -1e30


def layer_norm(summed, gain):
    center = jnp.mean(summed, axis=-1, keepdims=True)
    spread = jnp.mean(summed * summed, axis=-1, keepdims=True) - center * center
    return (summed - center) * lax.rsqrt(spread + EPSILON) * gain


def global_max(local_max, size):
    result = local_max
    distance = 1
    while distance < size:
        pairs = [(i, i ^ distance) for i in range(size)]
        result = jnp.maximum(result, lax.ppermute(result, "seq", pairs))
        distance *= 2
    return result


def global_totals(denom, numer):
    packed = jnp.concatenate([numer.reshape(-1), denom.reshape(-1)])
    packed = lax.psum(packed, "seq")
    count = numer.size
    return (packed[count:].reshape(denom.shape), packed[:count].reshape(numer.shape))


def reduce_norm(residual, partial_value, gain):
    width = residual.shape[1]
    total = lax.psum(partial_value, "tensor")
    full = layer_norm(residual.astype(jnp.float32) + total, gain).astype(jnp.bfloat16)
    columns = width // lax.axis_size("tensor")
    return (full, lax.dynamic_slice_in_dim(full, lax.axis_index("tensor") * columns, columns, 1))


def on_device(
    new_states,
    self_query,
    self_key,
    self_value,
    self_output,
    cross_query,
    cross_output,
    feed_up,
    feed_down,
    norm_self,
    norm_cross,
    norm_feed,
    self_cache,
    cross_cache,
    cache_lengths,
    page_table,
    request_order,
    encoder_lengths,
):
    states = lax.all_gather(new_states, "tensor", axis=2, tiled=True)
    steps, requests, width = states.shape
    flat = states.reshape(steps * requests, width)
    local_width = self_query.shape[1]
    local_heads = local_width // HEAD_DIM
    scaling = HEAD_DIM ** (-0.5)
    queries = (jnp.dot(flat, self_query, preferred_element_type=jnp.float32) * scaling).astype(
        jnp.bfloat16
    )
    new_keys = jnp.dot(flat, self_key, preferred_element_type=jnp.float32).astype(jnp.bfloat16)
    new_values = jnp.dot(flat, self_value, preferred_element_type=jnp.float32).astype(jnp.bfloat16)
    query_grid = queries.reshape(steps, requests, local_heads, HEAD_DIM)
    key_grid = new_keys.reshape(steps, requests, local_heads, HEAD_DIM)
    value_grid = new_values.reshape(steps, requests, local_heads, HEAD_DIM)
    slot_count = self_cache.shape[0]
    page_width = self_cache.shape[2]
    max_pages = page_table.shape[1]
    seq_index = lax.axis_index("seq")
    seq_size = lax.axis_size("seq")
    flat_table = page_table.reshape(-1)
    entry_ids = jnp.arange(requests * max_pages, dtype=jnp.int32)
    entry_request = entry_ids // max_pages
    entry_page = entry_ids % max_pages
    slot_ids = seq_index * slot_count + jnp.arange(slot_count, dtype=jnp.int32)
    matches = flat_table[None, :] == slot_ids[:, None]
    slot_live = jnp.any(matches, axis=1)
    slot_owner = jnp.sum(jnp.where(matches, entry_request[None, :], 0), axis=1)
    slot_page = jnp.sum(jnp.where(matches, entry_page[None, :], 0), axis=1)
    request_ids = jnp.arange(requests, dtype=jnp.int32)
    slot_length = jnp.sum(
        jnp.where(slot_owner[:, None] == request_ids[None, :], cache_lengths[None, :], 0), axis=1
    )
    positions = slot_page[:, None] * page_width + jnp.arange(page_width, dtype=jnp.int32)[None, :]
    slot_valid = slot_live[:, None] & (positions < slot_length[:, None])
    slot_rows = slot_live[:, None] & (request_order[None, :] == slot_owner[:, None])
    rows_half = slot_rows.astype(jnp.bfloat16)
    rows_wide = slot_rows.astype(jnp.float32)
    slot_query = jnp.einsum(
        "pb,sbc->psc",
        rows_half,
        queries.reshape(steps, requests, local_width),
        preferred_element_type=jnp.float32,
    ).astype(jnp.bfloat16)
    slot_query = slot_query.reshape(slot_count, steps, local_heads, HEAD_DIM)
    cache_keys = self_cache[:, 0].reshape(slot_count, page_width, local_heads, HEAD_DIM)
    cache_values = self_cache[:, 1].reshape(slot_count, page_width, local_heads, HEAD_DIM)
    cache_scores = jnp.einsum(
        "pshd,pkhd->pshk", slot_query, cache_keys, preferred_element_type=jnp.float32
    )
    valid_grid = slot_valid[:, None, None, :]
    slot_max = jnp.max(jnp.where(valid_grid, cache_scores, NEG_FILL), axis=3)
    row_max = jnp.max(
        jnp.where(slot_rows[:, None, :, None], slot_max[:, :, None, :], NEG_FILL), axis=0
    )
    causal = jnp.arange(steps)[None, :] <= jnp.arange(steps)[:, None]
    new_scores = jnp.einsum(
        "tbhd,ubhd->bhtu", query_grid, key_grid, preferred_element_type=jnp.float32
    )
    new_scores = jnp.where(causal, new_scores, NEG_FILL)
    new_max = jnp.transpose(jnp.max(new_scores, axis=3), (2, 0, 1))
    top = global_max(jnp.maximum(row_max, new_max), seq_size)
    slot_top = jnp.einsum("pb,sbh->psh", rows_wide, top, precision=lax.Precision.HIGHEST)
    cache_weights = jnp.exp(jnp.where(valid_grid, cache_scores - slot_top[..., None], NEG_FILL))
    cache_denom = jnp.sum(cache_weights, axis=3)
    cache_numer = jnp.einsum(
        "pshk,pkhd->pshd",
        cache_weights.astype(jnp.bfloat16),
        cache_values,
        preferred_element_type=jnp.float32,
    )
    row_denom = jnp.einsum("pb,psh->sbh", rows_wide, cache_denom, precision=lax.Precision.HIGHEST)
    row_numer = jnp.einsum("pb,pshd->sbhd", rows_wide, cache_numer, precision=lax.Precision.HIGHEST)
    total_denom, total_numer = global_totals(row_denom, row_numer)
    top_new = jnp.transpose(top, (1, 2, 0))[..., None]
    new_weights = jnp.where(causal, jnp.exp(new_scores - top_new), 0.0)
    new_denom = jnp.transpose(jnp.sum(new_weights, axis=3), (2, 0, 1))
    new_numer = jnp.einsum(
        "bhtu,ubhd->tbhd",
        new_weights.astype(jnp.bfloat16),
        value_grid,
        preferred_element_type=jnp.float32,
    )
    self_attn = ((total_numer + new_numer) / (total_denom + new_denom)[..., None]).astype(
        jnp.bfloat16
    )
    partial_value = jnp.dot(
        self_attn.reshape(steps * requests, local_width),
        self_output,
        preferred_element_type=jnp.float32,
    )
    first_full, first_share = reduce_norm(flat, partial_value, norm_self)
    cross_queries = (
        jnp.dot(first_full, cross_query, preferred_element_type=jnp.float32) * scaling
    ).astype(jnp.bfloat16)
    cross_grid = cross_queries.reshape(steps, requests, local_heads, HEAD_DIM)
    order_rows = (request_order[:, None] == request_ids[None, :]).astype(jnp.bfloat16)
    request_query = jnp.einsum(
        "br,sbhd->srhd", order_rows, cross_grid, preferred_element_type=jnp.float32
    ).astype(jnp.bfloat16)
    enc_local = cross_cache.shape[2]
    enc_keys = cross_cache[:, 0].reshape(requests, enc_local, local_heads, HEAD_DIM)
    enc_values = cross_cache[:, 1].reshape(requests, enc_local, local_heads, HEAD_DIM)
    enc_positions = seq_index * enc_local + jnp.arange(enc_local, dtype=jnp.int32)
    enc_valid = (enc_positions[None, :] < encoder_lengths[:, None])[None, :, None, :]
    enc_scores = jnp.einsum(
        "srhd,rehd->srhe", request_query, enc_keys, preferred_element_type=jnp.float32
    )
    enc_top = global_max(jnp.max(jnp.where(enc_valid, enc_scores, NEG_FILL), axis=3), seq_size)
    enc_weights = jnp.exp(jnp.where(enc_valid, enc_scores - enc_top[..., None], NEG_FILL))
    enc_numer_local = jnp.einsum(
        "srhe,rehd->srhd",
        enc_weights.astype(jnp.bfloat16),
        enc_values,
        preferred_element_type=jnp.float32,
    )
    enc_denom, enc_numer = global_totals(jnp.sum(enc_weights, axis=3), enc_numer_local)
    enc_attn = (enc_numer / enc_denom[..., None]).astype(jnp.bfloat16)
    cross_attn = jnp.einsum(
        "br,srhd->sbhd", order_rows, enc_attn, preferred_element_type=jnp.float32
    ).astype(jnp.bfloat16)
    partial_value = jnp.dot(
        cross_attn.reshape(steps * requests, local_width),
        cross_output,
        preferred_element_type=jnp.float32,
    )
    second_full, second_share = reduce_norm(first_full, partial_value, norm_cross)
    ffn_hidden = jax.nn.gelu(
        jnp.dot(second_full, feed_up, preferred_element_type=jnp.float32), approximate=False
    ).astype(jnp.bfloat16)
    ignored, out_share = reduce_norm(
        second_full, jnp.dot(ffn_hidden, feed_down, preferred_element_type=jnp.float32), norm_feed
    )
    return out_share.reshape(steps, requests, out_share.shape[1])


def solution(mesh):
    in_specs = (
        P(None, None, "tensor"),
        P(None, "tensor"),
        P(None, "tensor"),
        P(None, "tensor"),
        P("tensor", None),
        P(None, "tensor"),
        P("tensor", None),
        P(None, "tensor"),
        P("tensor", None),
        P(),
        P(),
        P(),
        P("seq", None, None, "tensor"),
        P(None, None, "seq", "tensor"),
        P(),
        P(),
        P(),
        P(),
    )
    out_specs = P(None, None, "tensor")
    return jax.shard_map(
        on_device, mesh=mesh, in_specs=in_specs, out_specs=out_specs, check_vma=False
    )
```

profile of v0, /device:TPU:1, one launch (start us, length us, event | category | flops | bytes accessed | tf_op | source)
XLA Modules:
  0.0 771.3 jit_solution(12482341161338022725)
XLA Ops:
  7.3 3.9 fusion.133
  11.2 2.6 copy.115
  15.2 24.1 %all-gather.2.cloned.1.call-done = bf16[4,128,1024]{2,1,0:T(8,128)(2,1)} async-done(((bf16[4,128,256]{2,1,0:T(8,128)(2,1)}), bf16[4,128,1024]{2,1,0:T(8,128)(2,1)}) %all-gather.2.cloned.1.call-update) | async-done | bytes 1048592 | tf_op jit(solution)/shard_map/all_gather | solution.py:62
  48.7 3.0 fusion.61
  59.2 2.7 collective-permute-start.2
  68.0 2.6 copy.164
  70.6 4.0 collective-permute-start.5
  93.8 179.4 %all-reduce.6.cloned.1.call-done = f32[133120]{0:T(1024)} async-done(((f32[133120]{0:T(1024)}), f32[133120]{0:T(1024)}) %all-reduce.6.cloned.1.call-update) | async-done | bytes 532496 | tf_op jit(solution)/shard_map/psum | solution.py:29
  291.5 3.4 copy.145
  294.9 55.6 %all-reduce.8.cloned.1.call-done = f32[512,1024]{1,0:T(8,128)} async-done(((f32[512,1024]{1,0:T(8,128)}), f32[512,1024]{1,0:T(8,128)}) %all-reduce.8.cloned.1.call-update) | async-done | bytes 2097168 | tf_op jit(solution)/shard_map/psum | solution.py:36
  358.2 3.2 select_reduce_fusion
  364.9 6.3 collective-permute-done.7
  371.2 2.8 collective-permute-start.8
  374.1 5.4 collective-permute-done.8
  380.9 4.5 collective-permute-done.9
  387.8 11.5 %collective-permute-done.10 = f32[4,128,4]{0,2,1:T(4,128)S(1)} collective-permute-done((f32[4,128,4]{0,2,1:T(4,128)S(1)}, f32[4,128,4]{0,2,1:T(4,128)S(1)}, u32[]{:S(2)}, u32[]{:S(2)}) %collective-permute-start.10) | collective-permute-done | bytes 8224 | tf_op jit(solution)/shard_map/ppermute | solution.py:22
  399.4 6.2 collective-permute-start.11
  407.8 3.4 copy.147
  411.2 2.9 collective-permute-done.11
  424.8 2.5 reshape.280
  429.3 182.5 %all-reduce.10.cloned.1.call-done = f32[133120]{0:T(1024)} async-done(((f32[133120]{0:T(1024)}), f32[133120]{0:T(1024)}) %all-reduce.10.cloned.1.call-update) | async-done | bytes 532496 | tf_op jit(solution)/shard_map/psum | solution.py:29
  620.9 63.5 %all-reduce.12.cloned.1.call-done = f32[512,1024]{1,0:T(8,128)} async-done(((f32[512,1024]{1,0:T(8,128)}), f32[512,1024]{1,0:T(8,128)}) %all-reduce.12.cloned.1.call-update) | async-done | bytes 2097168 | tf_op jit(solution)/shard_map/psum | solution.py:36
  688.0 9.5 %fusion.16 = f32[512,1024]{1,0:T(8,128)} fusion(bf16[1024,1024]{1,0:T(8,128)(2,1)S(1)} %copy-done, bf16[512,1024]{1,0:T(8,128)(2,1)} %multiply_convert_fusion, bf16[1024,1024]{1,0:T(8,128)(2,1)} %param.25), kind=kOutput, calls=%fused_computation.49 | convolution fusion | flops 2181562368 | bytes 7340032 | tf_op jit(solution)/shard_map/dot_general | solution.py:192
  698.4 62.9 %all-reduce.14.cloned.1.call-done = f32[512,1024]{1,0:T(8,128)} async-done(((f32[512,1024]{1,0:T(8,128)}), f32[512,1024]{1,0:T(8,128)}) %all-reduce.14.cloned.1.call-update) | async-done | bytes 2097168 | tf_op jit(solution)/shard_map/psum | solution.py:36
  (165 shorter events, 108.8 us)
Async XLA Ops:
  6.5 681.5 %copy-start = (bf16[1024,1024]{1,0:T(8,128)(2,1)S(1)}, bf16[1024,1024]{1,0:T(8,128)(2,1)}, u32[]{:S(2)}) copy-start(bf16[1024,1024]{1,0:T(8,128)(2,1)} %param.26) | copy-start | bytes 6291460
  6.5 32.7 %all-gather.2.cloned.1.call-start = ((), (), s32[]{:S(2)}) async-start(), calls=%async_computation | async-start | bytes 1310720 | tf_op jit(solution)/shard_map/all_gather | solution.py:62
  7.3 265.9 %all-reduce.6.cloned.1.call-start = ((), (), s32[]{:S(2)}) async-start(), calls=%async_computation.1 | async-start | bytes 1064960 | tf_op jit(solution)/shard_map/psum | solution.py:29
  11.2 28.1 %copy-start.17 = (bf16[1024,256]{1,0:T(8,128)(2,1)S(1)}, bf16[1024,256]{1,0:T(8,128)(2,1)}, u32[]{:S(2)}) copy-start(bf16[1024,256]{1,0:T(8,128)(2,1)} %param.19) | copy-start | bytes 1572868
  53.5 3.2 collective-permute-start
  56.7 2.5 collective-permute-start.1
  59.2 4.0 collective-permute-start.2
  63.2 2.5 collective-permute-start.3
  65.7 4.9 collective-permute-start.4
  70.6 8.2 %collective-permute-start.5 = (f32[4,128,4]{1,2,0:T(4,128)S(1)}, f32[4,128,4]{1,2,0:T(4,128)S(1)}, u32[]{:S(2)}, u32[]{:S(2)}) collective-permute-start(f32[4,128,4]{1,2,0:T(4,128)S(1)} %max.44), channel_id=1, source_target_pairs={{0,128},{4,132},{8,136},{12,140},{16,144},{20,148},{24,152},{28,15... | collective-permute-start | bytes 24584 | tf_op jit(solution)/shard_map/ppermute | solution.py:22
  88.6 261.9 %all-reduce.8.cloned.1.call-start = ((), (), s32[]{:S(2)}) async-start(), calls=%async_computation.2 | async-start | bytes 4194304 | tf_op jit(solution)/shard_map/psum | solution.py:36
  286.8 325.0 %all-reduce.10.cloned.1.call-start = ((), (), s32[]{:S(2)}) async-start(), calls=%async_computation.3 | async-start | bytes 1064960 | tf_op jit(solution)/shard_map/psum | solution.py:29
  286.9 63.7 %copy-start.4 = (bf16[4,128,1024]{2,1,0:T(8,128)(2,1)S(1)}, bf16[4,128,1024]{2,1,0:T(8,128)(2,1)}, u32[]{:S(2)}) copy-start(bf16[4,128,1024]{2,1,0:T(8,128)(2,1)} %all-gather.2.cloned.1.call-done) | copy-start | bytes 3145732
  291.5 61.3 %copy-start.14 = (f32[1024]{0:T(1024)S(1)}, f32[1024]{0:T(1024)}, u32[]{:S(2)}) copy-start(f32[1024]{0:T(1024)} %param.27) | copy-start | bytes 12292
  361.4 2.1 collective-permute-start.6
  363.6 7.6 collective-permute-start.7
  371.2 8.2 %collective-permute-start.8 = (f32[4,128,4]{0,2,1:T(4,128)S(1)}, f32[4,128,4]{0,2,1:T(4,128)S(1)}, u32[]{:S(2)}, u32[]{:S(2)}) collective-permute-start(f32[4,128,4]{0,2,1:T(4,128)S(1)} %max.47), channel_id=1, source_target_pairs={{0,16},{4,20},{8,24},{12,28},{16,0},{20,4},{24,8},{28,12},{32,48},... | collective-permute-start | bytes 24584 | tf_op jit(solution)/shard_map/ppermute | solution.py:22
  379.5 5.9 collective-permute-start.9
  385.5 13.8 %collective-permute-start.10 = (f32[4,128,4]{0,2,1:T(4,128)S(1)}, f32[4,128,4]{0,2,1:T(4,128)S(1)}, u32[]{:S(2)}, u32[]{:S(2)}) collective-permute-start(f32[4,128,4]{0,2,1:T(4,128)S(1)} %max.49), channel_id=1, source_target_pairs={{0,64},{4,68},{8,72},{12,76},{16,80},{20,84},{24,88},{28,92},{32,9... | collective-permute-start | bytes 24584 | tf_op jit(solution)/shard_map/ppermute | solution.py:22
  399.4 14.7 %collective-permute-start.11 = (f32[4,128,4]{0,2,1:T(4,128)S(1)}, f32[4,128,4]{0,2,1:T(4,128)}, u32[]{:S(2)}, u32[]{:S(2)}) collective-permute-start(f32[4,128,4]{0,2,1:T(4,128)S(1)} %max.50), channel_id=1, source_target_pairs={{0,128},{4,132},{8,136},{12,140},{16,144},{20,148},{24,152},{28,15... | collective-permute-start | bytes 24584 | tf_op jit(solution)/shard_map/ppermute | solution.py:22
  429.2 255.1 %all-reduce.12.cloned.1.call-start = ((), (), s32[]{:S(2)}) async-start(), calls=%async_computation.4 | async-start | bytes 4194304 | tf_op jit(solution)/shard_map/psum | solution.py:36
  620.6 65.9 %copy-start.15 = (f32[1024]{0:T(1024)S(1)}, f32[1024]{0:T(1024)}, u32[]{:S(2)}) copy-start(f32[1024]{0:T(1024)} %param.28) | copy-start | bytes 12292
  620.6 140.6 %all-reduce.14.cloned.1.call-start = ((), (), s32[]{:S(2)}) async-start(), calls=%async_computation.5 | async-start | bytes 4194304 | tf_op jit(solution)/shard_map/psum | solution.py:36
  697.5 63.8 %copy-start.6 = (bf16[512,1024]{1,0:T(8,128)(2,1)S(1)}, bf16[512,1024]{1,0:T(8,128)(2,1)}, u32[]{:S(2)}) copy-start(bf16[512,1024]{1,0:T(8,128)(2,1)} %multiply_convert_fusion) | copy-start | bytes 3145732
  (16 other events, 54.8 us)
Sparse Core Ops, SparseCore 0:
  9.1 30.0 all-gather.1
  88.8 184.3 all-reduce.5
  286.9 63.5 all-reduce.7
  429.4 182.3 all-reduce.9
  620.8 63.5 all-reduce.11
  697.6 63.5 all-reduce.13
where the time goes:
time: 781 us; the launch traced here: 771 us
  waiting for transfers between devices  605 us (77%)
  local copies, waits for them, and re-layouts  61.7 us (8%)
  matrix products  38.2 us (5%)
  starting transfers between devices  29.7 us (4%)
  other arithmetic  22.4 us (3%)
  between operations  14.1 us (2%)
    psum x2, waiting for transfers between devices, global_totals(): packed = lax.psum(packed, 'seq')  362 us
    psum x3, waiting for transfers between devices, reduce_norm(): total = lax.psum(partial_value, 'tensor')  182 us
    ppermute x12, waiting for transfers between devices, global_max(): result = jnp.maximum(result, lax.ppermute(result, 'seq', pairs))  36.4 us
    ppermute x12, starting transfers between devices, global_max(): result = jnp.maximum(result, lax.ppermute(result, 'seq', pairs))  28.8 us
    all_gather x1, waiting for transfers between devices, on_device(): states = lax.all_gather(new_states, 'tensor', axis=2, tiled=True)  24.1 us
  transfers between devices with their start and end apart: 18, of which 16 were waited for; matrix products, arithmetic and copies ran while one was open for 4% of the time, Pallas kernels for 0%

commit v1 on v0

--- a/solution.py
+++ b/solution.py
@@ -33,7 +33,9 @@
 
 def reduce_norm(residual, partial_value, gain):
     width = residual.shape[1]
-    total = lax.psum(partial_value, "tensor")
+    total = partial_value
+    for hop in (1, 2):
+        total = total + lax.ppermute(total, "tensor", [(dev, dev ^ hop) for dev in range(4)])
     full = layer_norm(residual.astype(jnp.float32) + total, gain).astype(jnp.bfloat16)
     columns = width // lax.axis_size("tensor")
     return (full, lax.dynamic_slice_in_dim(full, lax.axis_index("tensor") * columns, columns, 1))

time: 781 us -> 864 us (1.11)
  the two profiles are of different devices: /device:TPU:1 before, /device:TPU:128 now
where the time goes in v1:
time: 864 us; the launch traced here: 855 us
  waiting for transfers between devices  712 us (82%)
  local copies, waits for them, and re-layouts  47.2 us (5%)
  matrix products  33.4 us (4%)
  other arithmetic  26.6 us (3%)
  starting transfers between devices  22.2 us (3%)
  between operations  13.8 us (2%)
    psum x2, waiting for transfers between devices, global_totals(): packed = lax.psum(packed, 'seq')  356 us
    ppermute x6, waiting for transfers between devices, reduce_norm(): lax.ppermute(total, 'tensor', [(dev, dev ^ hop) for dev in range(4)])  270 us
    ppermute x12, waiting for transfers between devices, global_max(): result = jnp.maximum(result, lax.ppermute(result, 'seq', pairs))  61.7 us
    all_gather x1, waiting for transfers between devices, on_device(): states = lax.all_gather(new_states, 'tensor', axis=2, tiled=True)  23.4 us
  transfers between devices with their start and end apart: 21, of which 21 were waited for; matrix products, arithmetic and copies ran while one was open for 3% of the time, Pallas kernels for 0%

profile of v1, /device:TPU:128, one launch (start us, length us, event | category | flops | bytes accessed | tf_op | source)
XLA Modules:
  0.0 855.1 jit_solution(4368770984354838285)
XLA Ops:
  7.3 3.9 fusion.134
  15.2 23.4 %all-gather.2.cloned.1.call-done = bf16[4,128,1024]{2,1,0:T(8,128)(2,1)} async-done(((bf16[4,128,256]{2,1,0:T(8,128)(2,1)}), bf16[4,128,1024]{2,1,0:T(8,128)(2,1)}) %all-gather.2.cloned.1.call-update) | async-done | bytes 1048592 | tf_op jit(solution)/shard_map/all_gather | solution.py:64
  57.8 3.0 collective-permute-start.2
  63.6 3.0 collective-permute-done.3
  93.9 175.8 %all-reduce.3.cloned.1.call-done = f32[133120]{0:T(1024)} async-done(((f32[133120]{0:T(1024)}), f32[133120]{0:T(1024)}) %all-reduce.3.cloned.1.call-update) | async-done | bytes 532496 | tf_op jit(solution)/shard_map/psum | solution.py:29
  279.9 46.9 %collective-permute-done.6 = f32[512,1024]{1,0:T(8,128)S(1)} collective-permute-done((f32[512,1024]{1,0:T(8,128)S(1)}, f32[512,1024]{1,0:T(8,128)S(1)}, u32[]{:S(2)}, u32[]{:S(2)}) %collective-permute-start.6) | collective-permute-done | bytes 2097184 | tf_op jit(solution)/shard_map/ppermute | solution.py:38
  328.6 3.0 collective-permute-start.7
  337.8 40.2 %collective-permute-done.7 = f32[512,1024]{1,0:T(8,128)} collective-permute-done((f32[512,1024]{1,0:T(8,128)}, f32[512,1024]{1,0:T(8,128)}, u32[]{:S(2)}, u32[]{:S(2)}) %collective-permute-start.7) | collective-permute-done | bytes 2097184 | tf_op jit(solution)/shard_map/ppermute | solution.py:38
  383.9 3.1 select_reduce_fusion
  388.8 8.3 collective-permute-done.9
  397.7 8.6 %collective-permute-done.10 = f32[4,128,4]{0,2,1:T(4,128)S(1)} collective-permute-done((f32[4,128,4]{0,2,1:T(4,128)S(1)}, f32[4,128,4]{0,2,1:T(4,128)S(1)}, u32[]{:S(2)}, u32[]{:S(2)}) %collective-permute-start.10) | collective-permute-done | bytes 8224 | tf_op jit(solution)/shard_map/ppermute | solution.py:22
  406.6 6.6 collective-permute-done.11
  413.4 12.3 %collective-permute-done.12 = f32[4,128,4]{0,2,1:T(4,128)S(1)} collective-permute-done((f32[4,128,4]{0,2,1:T(4,128)S(1)}, f32[4,128,4]{0,2,1:T(4,128)S(1)}, u32[]{:S(2)}, u32[]{:S(2)}) %collective-permute-start.12) | collective-permute-done | bytes 8224 | tf_op jit(solution)/shard_map/ppermute | solution.py:22
  428.8 11.9 %collective-permute-done.13 = f32[4,128,4]{0,2,1:T(4,128)} collective-permute-done((f32[4,128,4]{0,2,1:T(4,128)S(1)}, f32[4,128,4]{0,2,1:T(4,128)}, u32[]{:S(2)}, u32[]{:S(2)}) %collective-permute-start.13) | collective-permute-done | bytes 8224 | tf_op jit(solution)/shard_map/ppermute | solution.py:22
  450.0 180.2 %all-reduce.5.cloned.1.call-done = f32[133120]{0:T(1024)} async-done(((f32[133120]{0:T(1024)}), f32[133120]{0:T(1024)}) %all-reduce.5.cloned.1.call-update) | async-done | bytes 532496 | tf_op jit(solution)/shard_map/psum | solution.py:29
  637.2 46.9 %collective-permute-done.14 = f32[512,1024]{1,0:T(8,128)S(1)} collective-permute-done((f32[512,1024]{1,0:T(8,128)S(1)}, f32[512,1024]{1,0:T(8,128)S(1)}, u32[]{:S(2)}, u32[]{:S(2)}) %collective-permute-start.14) | collective-permute-done | bytes 2097184 | tf_op jit(solution)/shard_map/ppermute | solution.py:38
  684.5 3.3 collective-permute-start.15
  687.8 46.2 %collective-permute-done.15 = f32[512,1024]{1,0:T(8,128)S(1)} collective-permute-done((f32[512,1024]{1,0:T(8,128)S(1)}, f32[512,1024]{1,0:T(8,128)S(1)}, u32[]{:S(2)}, u32[]{:S(2)}) %collective-permute-start.15) | collective-permute-done | bytes 2097184 | tf_op jit(solution)/shard_map/ppermute | solution.py:38
  735.9 9.8 %fusion.16 = f32[512,1024]{1,0:T(8,128)} fusion(bf16[1024,1024]{1,0:T(8,128)(2,1)S(1)} %copy-done, bf16[1024,1024]{1,0:T(8,128)(2,1)} %param.25, f32[512,1024]{1,0:T(8,128)} %get-tuple-element.14, f32[1024]{0:T(1024)S(1)} %copy-done.11, f32[512]{0:T(512)S(1)} %get-tuple-element.25, f32[512]{0:T(512)S(1)} %get-tuple-element.24), kind=kOutput, calls=%fused_computation.49 | convolution fusion | flops 2183659520 | bytes 8396800 | tf_op jit(solution)/shard_map/dot_general | solution.py:194
  747.2 45.5 %collective-permute-done.16 = f32[512,1024]{1,0:T(8,128)S(1)} collective-permute-done((f32[512,1024]{1,0:T(8,128)}, f32[512,1024]{1,0:T(8,128)S(1)}, u32[]{:S(2)}, u32[]{:S(2)}) %collective-permute-start.16) | collective-permute-done | bytes 2097184 | tf_op jit(solution)/shard_map/ppermute | solution.py:38
  792.7 3.3 add.137
  796.0 3.0 collective-permute-start.17
  799.7 44.0 %collective-permute-done.17 = f32[512,1024]{1,0:T(8,128)} collective-permute-done((f32[512,1024]{1,0:T(8,128)}, f32[512,1024]{1,0:T(8,128)}, u32[]{:S(2)}, u32[]{:S(2)}) %collective-permute-start.17) | collective-permute-done | bytes 2097184 | tf_op jit(solution)/shard_map/ppermute | solution.py:38
  843.8 3.6 fusion.131
  (160 shorter events, 105.2 us)
Async XLA Ops:
  6.5 729.3 %copy-start = (bf16[1024,1024]{1,0:T(8,128)(2,1)S(1)}, bf16[1024,1024]{1,0:T(8,128)(2,1)}, u32[]{:S(2)}) copy-start(bf16[1024,1024]{1,0:T(8,128)(2,1)} %param.26) | copy-start | bytes 6291460
  6.5 32.1 %all-gather.2.cloned.1.call-start = ((), (), s32[]{:S(2)}) async-start(), calls=%async_computation | async-start | bytes 1310720 | tf_op jit(solution)/shard_map/all_gather | solution.py:64
  7.3 262.4 %all-reduce.3.cloned.1.call-start = ((), (), s32[]{:S(2)}) async-start(), calls=%async_computation.1 | async-start | bytes 1064960 | tf_op jit(solution)/shard_map/psum | solution.py:29
  52.8 1.3 collective-permute-start
  54.1 3.7 collective-permute-start.1
  57.8 5.2 collective-permute-start.2
  62.9 3.7 collective-permute-start.3
  66.6 4.7 collective-permute-start.4
  71.3 7.6 collective-permute-start.5
  88.7 541.5 %all-reduce.5.cloned.1.call-start = ((), (), s32[]{:S(2)}) async-start(), calls=%async_computation.2 | async-start | bytes 1064960 | tf_op jit(solution)/shard_map/psum | solution.py:29
  278.3 48.5 %collective-permute-start.6 = (f32[512,1024]{1,0:T(8,128)S(1)}, f32[512,1024]{1,0:T(8,128)S(1)}, u32[]{:S(2)}, u32[]{:S(2)}) collective-permute-start(f32[512,1024]{1,0:T(8,128)S(1)} %fusion.69), channel_id=1, source_target_pairs={{0,1},{1,0},{2,3},{3,2},{4,5},{5,4},{6,7},{7,6},{8,9},{9,8},{10,11... | collective-permute-start | bytes 6291464 | tf_op jit(solution)/shard_map/ppermute | solution.py:38
  328.6 49.5 %collective-permute-start.7 = (f32[512,1024]{1,0:T(8,128)}, f32[512,1024]{1,0:T(8,128)}, u32[]{:S(2)}, u32[]{:S(2)}) collective-permute-start(f32[512,1024]{1,0:T(8,128)} %add.127), channel_id=1, source_target_pairs={{0,2},{1,3},{2,0},{3,1},{4,6},{5,7},{6,4},{7,5},{8,10},{9,11},{10,... | collective-permute-start | bytes 6291464 | tf_op jit(solution)/shard_map/ppermute | solution.py:38
  387.0 1.6 collective-permute-start.8
  388.7 8.4 collective-permute-start.9
  397.2 9.1 %collective-permute-start.10 = (f32[4,128,4]{0,2,1:T(4,128)S(1)}, f32[4,128,4]{0,2,1:T(4,128)S(1)}, u32[]{:S(2)}, u32[]{:S(2)}) collective-permute-start(f32[4,128,4]{0,2,1:T(4,128)S(1)} %max.47), channel_id=1, source_target_pairs={{0,16},{4,20},{8,24},{12,28},{16,0},{20,4},{24,8},{28,12},{32,48},... | collective-permute-start | bytes 24584 | tf_op jit(solution)/shard_map/ppermute | solution.py:22
  406.3 6.9 collective-permute-start.11
  413.3 12.4 %collective-permute-start.12 = (f32[4,128,4]{0,2,1:T(4,128)S(1)}, f32[4,128,4]{0,2,1:T(4,128)S(1)}, u32[]{:S(2)}, u32[]{:S(2)}) collective-permute-start(f32[4,128,4]{0,2,1:T(4,128)S(1)} %max.49), channel_id=1, source_target_pairs={{0,64},{4,68},{8,72},{12,76},{16,80},{20,84},{24,88},{28,92},{32,9... | collective-permute-start | bytes 24584 | tf_op jit(solution)/shard_map/ppermute | solution.py:22
  425.8 15.0 %collective-permute-start.13 = (f32[4,128,4]{0,2,1:T(4,128)S(1)}, f32[4,128,4]{0,2,1:T(4,128)}, u32[]{:S(2)}, u32[]{:S(2)}) collective-permute-start(f32[4,128,4]{0,2,1:T(4,128)S(1)} %max.50), channel_id=1, source_target_pairs={{0,128},{4,132},{8,136},{12,140},{16,144},{20,148},{24,152},{28,15... | collective-permute-start | bytes 24584 | tf_op jit(solution)/shard_map/ppermute | solution.py:22
  635.6 98.4 %copy-start.2 = (f32[512,1024]{1,0:T(8,128)S(1)}, f32[512,1024]{1,0:T(8,128)}, u32[]{:S(2)}) copy-start(f32[512,1024]{1,0:T(8,128)} %copy-done.1) | copy-start | bytes 6291460
  635.6 48.5 %collective-permute-start.14 = (f32[512,1024]{1,0:T(8,128)S(1)}, f32[512,1024]{1,0:T(8,128)S(1)}, u32[]{:S(2)}, u32[]{:S(2)}) collective-permute-start(f32[512,1024]{1,0:T(8,128)S(1)} %fusion.66), channel_id=1, source_target_pairs={{0,1},{1,0},{2,3},{3,2},{4,5},{5,4},{6,7},{7,6},{8,9},{9,8},{10,11... | collective-permute-start | bytes 6291464 | tf_op jit(solution)/shard_map/ppermute | solution.py:38
  684.5 51.4 %copy-start.11 = (f32[1024]{0:T(1024)S(1)}, f32[1024]{0:T(1024)}, u32[]{:S(2)}) copy-start(f32[1024]{0:T(1024)} %param.28) | copy-start | bytes 12292
  684.5 49.5 %collective-permute-start.15 = (f32[512,1024]{1,0:T(8,128)S(1)}, f32[512,1024]{1,0:T(8,128)S(1)}, u32[]{:S(2)}, u32[]{:S(2)}) collective-permute-start(f32[512,1024]{1,0:T(8,128)S(1)} %add.133), channel_id=1, source_target_pairs={{0,2},{1,3},{2,0},{3,1},{4,6},{5,7},{6,4},{7,5},{8,10},{9,11},{10,... | collective-permute-start | bytes 6291464 | tf_op jit(solution)/shard_map/ppermute | solution.py:38
  745.7 47.0 %collective-permute-start.16 = (f32[512,1024]{1,0:T(8,128)}, f32[512,1024]{1,0:T(8,128)S(1)}, u32[]{:S(2)}, u32[]{:S(2)}) collective-permute-start(f32[512,1024]{1,0:T(8,128)} %fusion.16), channel_id=1, source_target_pairs={{0,1},{1,0},{2,3},{3,2},{4,5},{5,4},{6,7},{7,6},{8,9},{9,8},{10,11... | collective-permute-start | bytes 6291464 | tf_op jit(solution)/shard_map/ppermute | solution.py:38
  796.0 47.8 %collective-permute-start.17 = (f32[512,1024]{1,0:T(8,128)}, f32[512,1024]{1,0:T(8,128)}, u32[]{:S(2)}, u32[]{:S(2)}) collective-permute-start(f32[512,1024]{1,0:T(8,128)} %add.137), channel_id=1, source_target_pairs={{0,2},{1,3},{2,0},{3,1},{4,6},{5,7},{6,4},{7,5},{8,10},{9,11},{10,... | collective-permute-start | bytes 6291464 | tf_op jit(solution)/shard_map/ppermute | solution.py:38
  (14 other events, 174.6 us)
Sparse Core Ops, SparseCore 0:
  9.1 29.4 all-gather.1
  88.8 180.8 all-reduce.2
  450.1 179.9 all-reduce.4
